TPU v7x, 512 devices: a whole 4x4x16 slice. The times are simulated.
512 devices in a mesh: dp: 8 (over z_hi, core), dom: 64 (over x, z_lo, y).
Axes of the slice: x: 4, y: 4, z: 16 (z_hi: 4, z_lo: 4; z = z_hi * 4 + z_lo), core: 2. Of those that a mesh axis runs over, the one named last changes fastest.
Arguments:
- density: bfloat16 [8, 64, 512, 256], P('dp', None, 'dom'), may hold values from -6 to 6
- upstream: bfloat16 [8, 64, 512, 256], P('dp', None, 'dom'), may hold values from -6 to 6
- spectral_weight: float32 [2048, 64], P(('dp', 'dom')), may hold values from -0.5 to 0.5
- moment_one: float32 [2048, 64], P(('dp', 'dom')), may hold values from -128 to 128
- moment_two: float32 [2048, 64], P(('dp', 'dom')), may hold values from 256 to 4096
- skip_weight: bfloat16 [64, 64], replicated, may hold values from -0.75 to 0.75
- skip_bias: float32 [64], replicated, may hold values from -3 to 3
- mode_counts: int32 [8], replicated, may hold values from 8 to 16, as said below
Outputs:
- input_grad: bfloat16 [8, 64, 512, 256], P('dp', None, 'dom')
- new_weight: float32 [2048, 64], P(('dp', 'dom'))
- new_moment_one: float32 [2048, 64], P(('dp', 'dom'))
- new_moment_two: float32 [2048, 64], P(('dp', 'dom'))
Inputs may be any that keep to these rules, and one draw needn't show every extreme that they name: `mode_counts`: some entry equals 16.
All inputs are finite; a program needn't handle non-finite values.
Results may differ from a plain program's by a relative error of at most 0.0053.
Values may be sent and summed in bfloat16 or wider, within the bound.
No kernel may reach another device: no remote copies, remote signals or barrier semaphores. Data moves between devices by JAX's collectives and lax.ppermute only.
A program may use at most 64 MiB of HBM per device.

v0:
```python
import math
import jax
import jax.numpy as jnp
from jax import lax
from jax.sharding import PartitionSpec as P

MODES = 16
STEP = 10
learn_rate = 0.01
beta_first = 0.9
beta_second = 0.95
decay_rate = 0.1
epsilon = 1e-08


def joined_along(tiles, dim):
    dims = list(tiles.shape[1:])
    dims[dim] *= tiles.shape[0]
    return jnp.moveaxis(tiles, 0, dim).reshape(dims)


def copy_for_each(shard, axis):
    copies = jnp.broadcast_to(shard, (lax.axis_size(axis), *shard.shape))
    return lax.all_to_all(copies, axis, split_axis=0, concat_axis=0, tiled=True)


def collect(shard, axis, dim):
    return joined_along(copy_for_each(shard, axis), dim)


def in_one_piece(arrays, axis, split_dim, concat_dim, along):
    both = jnp.concatenate(arrays, axis=along)
    result, at, done = (
        lax.all_to_all(both, axis, split_axis=split_dim, concat_axis=concat_dim, tiled=True),
        0,
        [],
    )
    for a in arrays:
        done.append(lax.slice_in_dim(result, at, at + a.shape[along], axis=along))
        at += a.shape[along]
    return tuple(done)


def split_up(shard, dim, length):
    dims = shard.shape
    tiles = shard.reshape(*dims[:dim], length, dims[dim] // length, *dims[dim + 1 :])
    return jnp.moveaxis(tiles, dim, 0)


def sum_at_owner(shard, axis, dim):
    tiles = split_up(shard, dim, lax.axis_size(axis))
    arrived = lax.all_to_all(tiles, axis, split_axis=0, concat_axis=0, tiled=True)
    return arrived.astype(jnp.float32).sum(axis=0)


def summed_on_arrival(shard, axis, dim):
    length = lax.axis_size(axis)
    tiles = lax.all_to_all(split_up(shard, dim, length), axis, 0, 0, tiled=True)
    return jnp.sum(tiles, axis=0)


def axis_parts(count_xdim):
    freq_list = jnp.arange(MODES, dtype=jnp.int32)
    cell_list = jnp.arange(count_xdim, dtype=jnp.int32)
    phases = (
        jnp.mod(freq_list[:, None] * cell_list[None, :], count_xdim).astype(jnp.float32)
        / count_xdim
    )
    angles = 2.0 * math.pi * phases
    scaling = 1.0 / math.sqrt(count_xdim)
    return (
        (jnp.cos(angles) * scaling).astype(jnp.bfloat16),
        (jnp.sin(angles) * scaling).astype(jnp.bfloat16),
    )


def doubling_table():
    return jnp.where(jnp.arange(MODES, dtype=jnp.int32) > 0, 2.0, 1.0).astype(jnp.float32)


def gelu_slope(values):
    cumulative = 0.5 * (1.0 + lax.erf(values * 0.7071067811865476))
    bell_curve = jnp.exp(-0.5 * values * values) * 0.3989422804014327
    return cumulative + values * bell_curve


def forward_parts(field, cosines, sines):
    real_part = jnp.einsum("scxl,fx->slcf", field, cosines, preferred_element_type=jnp.float32)
    imag_part = -jnp.einsum("scxl,fx->slcf", field, sines, preferred_element_type=jnp.float32)
    return (real_part, imag_part)


def inverse_cells(values_real, values_imag, cosines, sines):
    first = jnp.einsum("slcf,fx->scxl", values_real, cosines, preferred_element_type=jnp.float32)
    second = jnp.einsum("slcf,fx->scxl", values_imag, sines, preferred_element_type=jnp.float32)
    return (first - second).astype(jnp.bfloat16)


def on_device(
    density, upstream, spectral_weight, moment_one, moment_two, skip_weight, skip_bias, mode_counts
):
    samples, channels, slab_rows, line_count = density.shape
    count_xdim = slab_rows * lax.axis_size("dom")
    cosines, sines = axis_parts(count_xdim)
    doubling = doubling_table()
    doubling_low = doubling.astype(jnp.bfloat16)
    counts_here = lax.dynamic_slice_in_dim(mode_counts, lax.axis_index("dp") * samples, samples, 0)
    keep_modes = (jnp.arange(MODES, dtype=jnp.int32)[None, :] < counts_here[:, None]).astype(
        jnp.float32
    )
    keep_wide = keep_modes[:, None, None, :]
    weight_short = spectral_weight.astype(jnp.bfloat16)
    weight_low = lax.all_gather(weight_short, ("dp", "dom"), axis=0, tiled=True)
    weight_low = weight_low.reshape(2, MODES, channels, channels)
    weight_real = weight_low[0]
    weight_imag = weight_low[1]
    density_lines, upstream_lines = in_one_piece((density, upstream), "dom", 3, 2, 0)
    real_part, imag_part = forward_parts(density_lines, cosines, sines)
    spec_real = real_part.astype(jnp.bfloat16)
    spec_imag = imag_part.astype(jnp.bfloat16)
    form = "slcf,fco->slof"
    mixed_real = jnp.einsum(
        form, spec_real, weight_real, preferred_element_type=jnp.float32
    ) - jnp.einsum(form, spec_imag, weight_imag, preferred_element_type=jnp.float32)
    mixed_imag = jnp.einsum(
        form, spec_imag, weight_real, preferred_element_type=jnp.float32
    ) + jnp.einsum(form, spec_real, weight_imag, preferred_element_type=jnp.float32)
    mixed_real = (mixed_real * keep_wide).astype(jnp.bfloat16) * doubling_low
    mixed_imag = (mixed_imag * keep_wide).astype(jnp.bfloat16) * doubling_low
    back_lines = inverse_cells(mixed_real, mixed_imag, cosines, sines)
    back_rows = lax.optimization_barrier(back_lines)
    skip_part = jnp.einsum(
        "oc,scxl->soxl", skip_weight, density_lines, preferred_element_type=jnp.float32
    )
    before = back_rows.astype(jnp.float32) + skip_part + skip_bias[None, :, None, None]
    gate_lines = (upstream_lines.astype(jnp.float32) * gelu_slope(before)).astype(jnp.bfloat16)
    grad_real, grad_imag = forward_parts(gate_lines, cosines, sines)
    scale = keep_wide * doubling
    grad_real = (grad_real * scale).astype(jnp.bfloat16)
    grad_imag = (grad_imag * scale).astype(jnp.bfloat16)
    outer = "slof,slcf->fco"
    part_real = jnp.einsum(
        outer, grad_real, spec_real, preferred_element_type=jnp.float32
    ) + jnp.einsum(outer, grad_imag, spec_imag, preferred_element_type=jnp.float32)
    part_imag = jnp.einsum(
        outer, grad_imag, spec_real, preferred_element_type=jnp.float32
    ) - jnp.einsum(outer, grad_real, spec_imag, preferred_element_type=jnp.float32)
    grad_local = jnp.stack([part_real, part_imag], 0).reshape(2 * MODES * channels, channels)
    weight_grad = lax.psum_scatter(grad_local, ("dp", "dom"), scatter_dimension=0, tiled=True)
    inner = "fco,slof->slcf"
    input_real = jnp.einsum(
        inner, weight_real, grad_real, preferred_element_type=jnp.float32
    ) + jnp.einsum(inner, weight_imag, grad_imag, preferred_element_type=jnp.float32)
    input_imag = jnp.einsum(
        inner, weight_real, grad_imag, preferred_element_type=jnp.float32
    ) - jnp.einsum(inner, weight_imag, grad_real, preferred_element_type=jnp.float32)
    input_lines = inverse_cells(
        input_real.astype(jnp.bfloat16), input_imag.astype(jnp.bfloat16), cosines, sines
    )
    input_rows = lax.optimization_barrier(input_lines)
    skip_back = jnp.einsum(
        "oc,soxl->scxl", skip_weight, gate_lines, preferred_element_type=jnp.float32
    )
    grad_lines = (input_rows.astype(jnp.float32) + skip_back).astype(jnp.bfloat16)
    input_grad = lax.all_to_all(grad_lines, "dom", split_axis=2, concat_axis=3, tiled=True)
    new_moment_one = beta_first * moment_one + (1.0 - beta_first) * weight_grad
    new_moment_two = beta_second * moment_two + (1.0 - beta_second) * weight_grad * weight_grad
    first_hat = new_moment_one / (1.0 - beta_first**STEP)
    second_hat = new_moment_two / (1.0 - beta_second**STEP)
    new_weight = spectral_weight - learn_rate * (
        first_hat / (jnp.sqrt(second_hat) + epsilon) + decay_rate * spectral_weight
    )
    return (input_grad, new_weight, new_moment_one, new_moment_two)


def solution(mesh):
    placed = (
        P("dp", None, "dom", None),
        P("dp", None, "dom", None),
        P(("dp", "dom"), None),
        P(("dp", "dom"), None),
        P(("dp", "dom"), None),
        P(),
        P(),
        P(),
    )
    return jax.shard_map(
        on_device,
        mesh=mesh,
        in_specs=placed,
        out_specs=(
            P("dp", None, "dom", None),
            P(("dp", "dom"), None),
            P(("dp", "dom"), None),
            P(("dp", "dom"), None),
        ),
        check_vma=False,
    )
```

profile of v0, /device:TPU:1, one launch (start us, length us, event | category | flops | bytes accessed | tf_op | source)
XLA Modules:
  0.0 1845.9 jit_solution(2929761174149622552)
XLA Ops:
  7.2 0.0 copy-start
  7.2 0.0 copy-start.1
  7.2 1.5 copy.68
  8.7 0.0 copy-done.1
  8.7 0.4 copy.67
  9.1 0.2 fusion.142
  9.3 1.5 reshape.169
  10.9 12.6 all-to-all-start
  23.5 0.0 copy-start.5
  23.5 0.6 copy-done.5
  24.1 0.6 dynamic_slice.3
  24.7 0.7 compare_convert_fusion
  25.4 0.7 compare_select_fusion.1
  26.0 0.0 copy-done.2
  26.1 1322.4 %all-gather = bf16[512,4,64]{2,1,0:T(4,128)(2,1)S(1)} all-gather(bf16[1,4,64]{2,1,0:T(4,128)(2,1)S(1)} %convert_bitcast_fusion), channel_id=1, replica_groups=mesh['dp'=8,'dom'=64] {'dp','dom'}, dimensions={0}, use_global_device_ids=true | all-gather | bytes 262656 | tf_op jit(solution)/shard_map/all_gather | solution.py:113
  1348.4 0.2 fusion.141
  1348.6 0.0 all-to-all-done
  1348.6 0.7 reshape.170
  1349.3 0.1 copy.69
  1349.4 0.2 fusion.140
  1349.6 0.3 fusion.32
  1349.9 0.3 fusion.33
  1350.1 0.1 copy.160
  1350.2 0.3 copy.81
  1350.5 0.2 fusion.95
  1350.7 0.2 fusion.89
  1350.9 0.2 fusion.30
  1351.1 0.3 fusion.65
  1351.4 0.2 fusion.31
  1351.6 0.0 copy-start.6
  1351.6 0.3 fusion.9
  1352.0 0.0 copy-done
  1352.0 0.3 copy-done.6
  1352.3 0.5 fusion.45
  1352.8 0.3 fusion.27
  1353.0 0.3 fusion.26
  1353.3 0.2 fusion.78
  1353.5 0.3 fusion.75
  1353.8 0.2 fusion.85
  1354.1 0.3 fusion.25
  1354.3 0.4 fusion.62
  1354.7 0.2 fusion.24
  1354.9 0.4 fusion.8
  1355.3 0.3 fusion.5
  1355.6 0.3 copy.89
  1355.9 1.0 reshape.171
  1356.9 4.6 all-to-all-start.1
  1361.5 0.0 all-reduce.3.cloned.1.call-start
  1361.6 0.3 fusion
  1361.9 0.3 fusion.82
  1362.1 0.3 fusion.1
  1362.4 1.1 pad_maximum_fusion.1
  1363.5 0.0 all-reduce.3.cloned.1.call-update
  1363.6 0.0 copy-start.3
  1363.6 0.0 copy-start.4
  1363.6 472.5 %all-reduce.3.cloned.1.call-done = f32[2048,64]{1,0:T(8,128)} async-done(((f32[2048,64]{1,0:T(8,128)}), f32[2048,64]{1,0:T(8,128)}) %all-reduce.3.cloned.1.call-update) | async-done | bytes 524304
  1836.1 0.0 copy-done.3
  1836.1 0.0 copy-done.4
  1836.1 1.3 multiply_subtract_fusion
  1837.4 0.0 all-to-all-done.1
  1837.4 0.3 reshape.172
  1837.7 0.1 copy.161
  1837.8 0.1 copy.91
  1837.9 1.1 copy.100
  (3 shorter events, 0.0 us)
Async XLA Ops:
  7.2 1344.8 %copy-start = (bf16[64,64]{1,0:T(8,128)(2,1)S(1)}, bf16[64,64]{1,0:T(8,128)(2,1)}, u32[]{:S(2)}) copy-start(bf16[64,64]{1,0:T(8,128)(2,1)} %param.13) | copy-start | bytes 24580
  7.2 1.5 copy-start.1
  10.9 1337.7 %all-to-all-start = ((bf16[64,2,2048]{2,1,0:T(2,128)(2,1)}), bf16[64,2,2048]{2,1,0:T(2,128)(2,1)S(1)}, u32[]{:S(2)}, u32[]{:S(2)}) async-start(bf16[64,2,2048]{2,1,0:T(2,128)(2,1)} %reshape.169), calls=%async_computation | async-start | bytes 1048576 | tf_op jit(solution)/shard_map/all_to_all | solution.py:34
  23.5 0.7 copy-start.5
  24.7 1.3 copy-start.2
  1351.6 0.7 copy-start.6
  1356.9 480.5 %all-to-all-start.1 = ((bf16[64,2,1024]{2,1,0:T(2,128)(2,1)}), bf16[64,2,1024]{2,1,0:T(2,128)(2,1)S(1)}, u32[]{:S(2)}, u32[]{:S(2)}) async-start(bf16[64,2,1024]{2,1,0:T(2,128)(2,1)} %reshape.171), calls=%async_computation.1 | async-start | bytes 524288 | tf_op jit(solution)/shard_map/all_to_all | solution.py:165
  1361.5 474.5 %all-reduce.3.cloned.1.call-start = ((), (), s32[]{:S(2)}) async-start(), calls=%async_computation.2 | async-start | bytes 2097152
  1363.6 472.5 %copy-start.3 = (f32[4,64]{1,0:T(4,128)S(1)}, f32[4,64]{1,0:T(4,128)}, u32[]{:S(2)}) copy-start(f32[4,64]{1,0:T(4,128)} %param.11) | copy-start | bytes 3076
  1363.6 472.5 %copy-start.4 = (f32[4,64]{1,0:T(4,128)S(1)}, f32[4,64]{1,0:T(4,128)}, u32[]{:S(2)}) copy-start(f32[4,64]{1,0:T(4,128)} %param.12) | copy-start | bytes 3076
Sparse Core Ops, SparseCore 0:
  1367.8 468.1 all-reduce.2
where the time goes:
time: 1850 us
  blocking collectives  1320 us (71%)
  waiting for transfers between devices  472 us (26%)
    all_gather x1, blocking collectives, on_device(): weight_low = lax.all_gather(weight_short, ('dp', 'dom'), axis=0, tiled=True)  1320 us
    unnamed x2, waiting for transfers between devices  472 us
  transfers between devices with their start and end apart: 3, of which 1 were waited for; matrix products, arithmetic and copies ran while one was open for 0% of the time, Pallas kernels for 0%

commit v1 on v0

--- a/solution.py
+++ b/solution.py
@@ -110,7 +110,12 @@
     )
     keep_wide = keep_modes[:, None, None, :]
     weight_short = spectral_weight.astype(jnp.bfloat16)
-    weight_low = lax.all_gather(weight_short, ("dp", "dom"), axis=0, tiled=True)
+    weight_low = jnp.concatenate(
+        lax.all_to_all(
+            jnp.stack([weight_short] * lax.axis_size(("dp", "dom"))), ("dp", "dom"), 0, 0
+        ),
+        axis=0,
+    )
     weight_low = weight_low.reshape(2, MODES, channels, channels)
     weight_real = weight_low[0]
     weight_imag = weight_low[1]

time: 1850 us -> 573 us (0.31)
  blocking collectives: 1320 us -> 0 us
  waiting for transfers between devices: 472 us -> 502 us
    all_gather x1 -> x0, blocking collectives: 1320 us -> none  [on_device(): weight_low = lax.all_gather(weight_short, ('dp', 'dom'), axis=0, tiled=True)]
    all_to_all x0 -> x1, starting transfers between devices: none -> 24.3 us  [on_device(): lax.all_to_all(jnp.stack([weight_short] * lax.axis_size(('dp', 'dom'))),...]
    all_to_all x0 -> x1, waiting for transfers between devices: none -> 21.2 us  [on_device(): lax.all_to_all(jnp.stack([weight_short] * lax.axis_size(('dp', 'dom'))),...]
  transfers between devices with their start and end apart: 3 -> 4, of which waited for: 1 -> 3; matrix products, arithmetic and copies ran while one was open for 0% -> 1% of each run, Pallas kernels for 0% -> 0%
where the time goes in v1:
time: 573 us; the launch traced here: 572 us
  waiting for transfers between devices  502 us (88%)
  starting transfers between devices  35.1 us (6%)
  between operations  14.3 us (2%)
  local copies, waits for them, and re-layouts  10 us (2%)
  matrix products  6.03 us (1%)
    unnamed x2, waiting for transfers between devices  466 us
    all_to_all x1, starting transfers between devices, on_device(): lax.all_to_all(jnp.stack([weight_short] * lax.axis_size(('dp', 'dom'))),...  24.3 us
    all_to_all x1, waiting for transfers between devices, on_device(): lax.all_to_all(jnp.stack([weight_short] * lax.axis_size(('dp', 'dom'))),...  21.2 us
    all_to_all x1, waiting for transfers between devices, in_one_piece(): lax.all_to_all(both, axis, split_axis=split_dim, concat_axis=concat_dim,...  14.2 us
  transfers between devices with their start and end apart: 4, of which 3 were waited for; matrix products, arithmetic and copies ran while one was open for 1% of the time, Pallas kernels for 0%

profile of v1, /device:TPU:1, one launch (start us, length us, event | category | flops | bytes accessed | tf_op | source)
XLA Modules:
  0.0 572.3 jit_solution(4308299857893684298)
XLA Ops:
  7.2 0.0 copy-start
  7.2 0.7 convert_element_type.165
  7.9 0.1 stack.8
  8.0 1.0 reshape.166
  9.0 24.3 %all-to-all-start.1 = ((bf16[512,2,128]{2,1,0:T(2,128)(2,1)}), bf16[512,2,128]{2,1,0:T(2,128)(2,1)S(1)}, u32[]{:S(2)}, u32[]{:S(2)}) async-start(bf16[512,2,128]{2,1,0:T(2,128)(2,1)} %reshape.166), calls=%async_computation.1 | async-start | bytes 524288 | tf_op jit(solution)/shard_map/all_to_all | solution.py:114
  33.3 0.0 copy-start.2
  33.3 0.4 copy.68
  33.7 0.5 copy-done.2
  34.2 0.4 copy.67
  34.7 0.2 fusion.142
  34.9 1.5 reshape.164
  36.4 21.2 %all-to-all-done.1 = bf16[512,2,128]{2,1,0:T(2,128)(2,1)S(1)} async-done(((bf16[512,2,128]{2,1,0:T(2,128)(2,1)}), bf16[512,2,128]{2,1,0:T(2,128)(2,1)S(1)}, u32[]{:S(2)}, u32[]{:S(2)}) %all-to-all-start.1) | async-done | bytes 262176 | tf_op jit(solution)/shard_map/all_to_all | solution.py:114
  57.7 5.3 all-to-all-start
  63.0 0.0 copy-start.6
  63.1 0.6 copy-done.6
  63.7 0.6 dynamic_slice.3
  64.3 0.6 compare_convert_fusion
  64.9 0.7 compare_select_fusion.1
  65.6 0.2 reshape.167
  65.8 0.2 fusion.141
  66.0 14.2 %all-to-all-done = bf16[64,2,2048]{2,1,0:T(2,128)(2,1)S(1)} async-done(((bf16[64,2,2048]{2,1,0:T(2,128)(2,1)}), bf16[64,2,2048]{2,1,0:T(2,128)(2,1)S(1)}, u32[]{:S(2)}, u32[]{:S(2)}) %all-to-all-start) | async-done | bytes 524320 | tf_op jit(solution)/shard_map/all_to_all | solution.py:34
  80.3 0.7 reshape.165
  80.9 0.1 copy.69
  81.0 0.2 fusion.140
  81.2 0.3 fusion.32
  81.5 0.3 fusion.33
  81.8 0.1 copy.160
  81.9 0.3 copy.81
  82.2 0.2 fusion.95
  82.4 0.2 fusion.89
  82.5 0.2 fusion.30
  82.7 0.3 fusion.65
  83.1 0.2 fusion.31
  83.3 0.0 copy-start.7
  83.3 0.3 fusion.9
  83.6 0.3 copy-done.7
  83.9 0.5 fusion.45
  84.4 0.3 fusion.27
  84.7 0.3 fusion.26
  84.9 0.2 fusion.78
  85.2 0.3 fusion.75
  85.5 0.2 fusion.85
  85.7 0.3 fusion.25
  86.0 0.4 fusion.62
  86.3 0.2 fusion.24
  86.6 0.4 fusion.8
  86.9 0.3 fusion.5
  87.2 0.3 copy.89
  87.5 1.0 reshape.168
  88.5 5.4 all-to-all-start.2
  93.9 0.0 all-reduce.3.cloned.1.call-start
  94.0 0.3 fusion
  94.3 0.3 fusion.82
  94.6 0.3 fusion.1
  94.9 1.1 pad_maximum_fusion.1
  96.0 0.0 all-reduce.3.cloned.1.call-update
  96.0 0.0 copy-start.3
  96.0 0.0 copy-start.4
  96.0 466.5 %all-reduce.3.cloned.1.call-done = f32[2048,64]{1,0:T(8,128)} async-done(((f32[2048,64]{1,0:T(8,128)}), f32[2048,64]{1,0:T(8,128)}) %all-reduce.3.cloned.1.call-update) | async-done | bytes 524304
  562.5 1.3 multiply_subtract_fusion
  563.8 0.3 reshape.169
  564.1 0.1 copy.161
  564.2 0.1 copy.91
  564.3 1.1 copy.100
  (9 shorter events, 0.0 us)
Async XLA Ops:
  7.2 76.5 %copy-start = (bf16[64,64]{1,0:T(8,128)(2,1)S(1)}, bf16[64,64]{1,0:T(8,128)(2,1)}, u32[]{:S(2)}) copy-start(bf16[64,64]{1,0:T(8,128)(2,1)} %param.13) | copy-start | bytes 24580
  9.0 24.3 %copy-start.1 = (bf16[1,64,8,256]{3,2,1,0:T(8,128)(2,1)S(1)}, bf16[1,64,8,256]{3,2,1,0:T(8,128)(2,1)}, u32[]{:S(2)}) copy-start(bf16[1,64,8,256]{3,2,1,0:T(8,128)(2,1)} %param.9) | copy-start | bytes 786436
  9.0 48.7 %all-to-all-start.1 = ((bf16[512,2,128]{2,1,0:T(2,128)(2,1)}), bf16[512,2,128]{2,1,0:T(2,128)(2,1)S(1)}, u32[]{:S(2)}, u32[]{:S(2)}) async-start(bf16[512,2,128]{2,1,0:T(2,128)(2,1)} %reshape.166), calls=%async_computation.1 | async-start | bytes 524288 | tf_op jit(solution)/shard_map/all_to_all | solution.py:114
  33.3 1.0 copy-start.2
  57.7 22.6 %all-to-all-start = ((bf16[64,2,2048]{2,1,0:T(2,128)(2,1)}), bf16[64,2,2048]{2,1,0:T(2,128)(2,1)S(1)}, u32[]{:S(2)}, u32[]{:S(2)}) async-start(bf16[64,2,2048]{2,1,0:T(2,128)(2,1)} %reshape.164), calls=%async_computation | async-start | bytes 1048576 | tf_op jit(solution)/shard_map/all_to_all | solution.py:34
  63.0 0.7 copy-start.6
  83.3 0.7 copy-start.7
  88.5 475.3 %all-to-all-start.2 = ((bf16[64,2,1024]{2,1,0:T(2,128)(2,1)}), bf16[64,2,1024]{2,1,0:T(2,128)(2,1)S(1)}, u32[]{:S(2)}, u32[]{:S(2)}) async-start(bf16[64,2,1024]{2,1,0:T(2,128)(2,1)} %reshape.168), calls=%async_computation.2 | async-start | bytes 524288 | tf_op jit(solution)/shard_map/all_to_all | solution.py:170
  93.9 468.6 %all-reduce.3.cloned.1.call-start = ((), (), s32[]{:S(2)}) async-start(), calls=%async_computation.3 | async-start | bytes 2097152
  96.0 466.5 %copy-start.5 = (f32[4,64]{1,0:T(4,128)S(1)}, f32[4,64]{1,0:T(4,128)}, u32[]{:S(2)}) copy-start(f32[4,64]{1,0:T(4,128)} %param.12) | copy-start | bytes 3076
  96.0 466.5 %copy-start.3 = (f32[4,64]{1,0:T(4,128)S(1)}, f32[4,64]{1,0:T(4,128)}, u32[]{:S(2)}) copy-start(f32[4,64]{1,0:T(4,128)} %param.10) | copy-start | bytes 3076
  96.0 466.5 %copy-start.4 = (f32[4,64]{1,0:T(4,128)S(1)}, f32[4,64]{1,0:T(4,128)}, u32[]{:S(2)}) copy-start(f32[4,64]{1,0:T(4,128)} %param.11) | copy-start | bytes 3076
Sparse Core Ops, SparseCore 0:
  100.2 462.2 all-reduce.2
